TPU v7x, 32 devices: a whole 2x2x4 slice. The times are simulated.
32 devices in a mesh: rep: 4 (over y, core), fsdp: 4 (over z), seq: 2 (over x).
Axes of the slice: x: 2, y: 2, z: 4, core: 2. Of those that a mesh axis runs over, the one named last changes fastest.
Arguments:
- tokens: bfloat16 [16, 1024, 1024], P(('rep', 'fsdp'), 'seq'), may hold values from -6 to 6
- positions: int32 [3, 16, 1024], P(None, ('rep', 'fsdp'), 'seq'), may hold values from 0 to 15
- input_gain: bfloat16 [1024], P('fsdp'), may hold values from 0.5 to 1.5
- input_shift: bfloat16 [1024], P('fsdp'), may hold values from -1.5 to 1.5
- joint_weight: bfloat16 [1024, 3072], P('fsdp'), may hold values from -0.1875 to 0.1875
- joint_bias: bfloat16 [3072], P('fsdp'), may hold values from -1.5 to 1.5
- output_weight: bfloat16 [1024, 1024], P('fsdp'), may hold values from -3 to 3
- output_bias: bfloat16 [1024], P('fsdp'), may hold values from -1.5 to 1.5
- middle_gain: bfloat16 [1024], P('fsdp'), may hold values from 0.5 to 1.5
- middle_shift: bfloat16 [1024], P('fsdp'), may hold values from -1.5 to 1.5
- expand_weight: bfloat16 [1024, 4096], P('fsdp'), may hold values from -0.1875 to 0.1875
- expand_bias: bfloat16 [4096], P('fsdp'), may hold values from -2.5 to 2.5
- reduce_weight: bfloat16 [4096, 1024], P('fsdp'), may hold values from -0.09375 to 0.09375
- reduce_bias: bfloat16 [1024], P('fsdp'), may hold values from -1.5 to 1.5
- cotangent: bfloat16 [16, 1024, 1024], P(('rep', 'fsdp'), 'seq'), may hold values from -6 to 6
Outputs:
- block_output: bfloat16 [16, 1024, 1024], P(('rep', 'fsdp'), 'seq')
- input_gradient: float32 [16, 1024, 1024], P(('rep', 'fsdp'), 'seq')
- input_gain_gradient: float32 [1024], P('fsdp')
- input_shift_gradient: float32 [1024], P('fsdp')
- joint_weight_gradient: float32 [1024, 3072], P('fsdp')
- joint_bias_gradient: float32 [3072], P('fsdp')
- output_weight_gradient: float32 [1024, 1024], P('fsdp')
- output_bias_gradient: float32 [1024], P('fsdp')
- middle_gain_gradient: float32 [1024], P('fsdp')
- middle_shift_gradient: float32 [1024], P('fsdp')
- expand_weight_gradient: float32 [1024, 4096], P('fsdp')
- expand_bias_gradient: float32 [4096], P('fsdp')
- reduce_weight_gradient: float32 [4096, 1024], P('fsdp')
- reduce_bias_gradient: float32 [1024], P('fsdp')
All inputs are finite; a program needn't handle non-finite values.
Results may differ from a plain program's by a relative error of at most 0.018.
Values may be sent and summed in bfloat16 or wider, within the bound.
No kernel may reach another device: no remote copies, remote signals or barrier semaphores. Data moves between devices by JAX's collectives and lax.ppermute only.
A program may use at most 192 MiB of HBM per device.

v0:
```python
import jax
import jax.numpy as jnp
from jax import lax
from jax.sharding import PartitionSpec as P

epsilon = 1e-06


def norm_rows(values, gains, shifts):
    average = jnp.mean(values, axis=-1, keepdims=True)
    centred = values - average
    spread = jnp.mean(centred * centred, axis=-1, keepdims=True)
    return centred * lax.rsqrt(spread + epsilon) * gains + shifts


def rotary_tables(positions):
    counter = jnp.arange(10).astype(jnp.float32)
    frequency = jnp.power(10000.0, -counter / 10.0)
    angles = positions.astype(jnp.float32)[:, :, None] * frequency
    angles = jnp.transpose(angles, (1, 0, 2))
    return (jnp.cos(angles), jnp.sin(angles))


def rotate(values, cosine_part, sine_part):
    length = values.shape[0]
    heads_count = values.shape[1]
    turned = values[:, :, :60].reshape(length, heads_count, 3, 2, 10)
    former = turned[:, :, :, 0, :]
    latter = turned[:, :, :, 1, :]
    cosine_wide = cosine_part[:, None, :, :]
    sine_wide = sine_part[:, None, :, :]
    new_former = former * cosine_wide - latter * sine_wide
    new_latter = latter * cosine_wide + former * sine_wide
    joined = jnp.stack([new_former, new_latter], axis=3).reshape(length, heads_count, 60)
    return jnp.concatenate([joined, values[:, :, 60:]], axis=2)


def exact_gelu(values):
    return jax.nn.gelu(values, approximate=False)


def split_heads(block):
    return block.reshape(block.shape[0], block.shape[1] // 64, 64)


def group_scores(query_heads, key_heads):
    return (
        jnp.einsum("thd,shd->hts", query_heads, key_heads, preferred_element_type=jnp.float32)
        * 0.125
    )


def attend(inputs):
    query_block, key_block, value_block = inputs
    query_heads = split_heads(query_block)
    key_heads = split_heads(key_block)
    value_heads = split_heads(value_block)
    scores = group_scores(query_heads, key_heads)
    row_max = jnp.max(scores, axis=2, keepdims=True)
    raised = jnp.exp(scores - row_max)
    row_total = jnp.sum(raised, axis=2, keepdims=True)
    probs_low = (raised / row_total).astype(jnp.bfloat16)
    mixed = jnp.einsum("hts,shd->thd", probs_low, value_heads, preferred_element_type=jnp.float32)
    return (mixed.reshape(query_block.shape[0], -1), row_max, row_total)


def attend_back(inputs):
    query_block, key_block, value_block, grad_block, row_max, row_total = inputs
    query_heads = split_heads(query_block)
    key_heads = split_heads(key_block)
    value_heads = split_heads(value_block)
    grad_heads = split_heads(grad_block)
    scores = group_scores(query_heads, key_heads)
    probs = jnp.exp(scores - row_max) / row_total
    probs_low = probs.astype(jnp.bfloat16)
    grad_probs = jnp.einsum(
        "thd,shd->hts", grad_heads, value_heads, preferred_element_type=jnp.float32
    )
    value_grad = jnp.einsum(
        "hts,thd->shd", probs_low, grad_heads, preferred_element_type=jnp.float32
    )
    inner = jnp.sum(grad_probs * probs, axis=2, keepdims=True)
    grad_scores = (probs * (grad_probs - inner)).astype(jnp.bfloat16)
    query_grad = (
        jnp.einsum("hts,shd->thd", grad_scores, key_heads, preferred_element_type=jnp.float32)
        * 0.125
    )
    key_grad = (
        jnp.einsum("hts,thd->shd", grad_scores, query_heads, preferred_element_type=jnp.float32)
        * 0.125
    )
    return (
        query_grad.reshape(query_block.shape[0], -1),
        key_grad.reshape(key_block.shape[0], -1),
        value_grad.reshape(key_block.shape[0], -1),
    )


def local(
    tokens,
    positions,
    input_gain,
    input_shift,
    joint_weight,
    joint_bias,
    output_weight,
    output_bias,
    middle_gain,
    middle_shift,
    expand_weight,
    expand_bias,
    reduce_weight,
    reduce_bias,
    cotangent,
):
    shards = (
        input_gain,
        input_shift,
        joint_weight,
        joint_bias,
        output_weight,
        output_bias,
        middle_gain,
        middle_shift,
        expand_weight,
        expand_bias,
        reduce_weight,
        reduce_bias,
    )
    gathered = (
        lax.all_gather(shards[0], "fsdp", axis=0, tiled=True),
        lax.all_gather(shards[1], "fsdp", axis=0, tiled=True),
        lax.all_gather(shards[2], "fsdp", axis=0, tiled=True),
        lax.all_gather(shards[3], "fsdp", axis=0, tiled=True),
        lax.all_gather(shards[4], "fsdp", axis=0, tiled=True),
        lax.all_gather(shards[5], "fsdp", axis=0, tiled=True),
        lax.all_gather(shards[6], "fsdp", axis=0, tiled=True),
        lax.all_gather(shards[7], "fsdp", axis=0, tiled=True),
        lax.all_gather(shards[8], "fsdp", axis=0, tiled=True),
        lax.all_gather(shards[9], "fsdp", axis=0, tiled=True),
        lax.all_gather(shards[10], "fsdp", axis=0, tiled=True),
        lax.all_gather(shards[11], "fsdp", axis=0, tiled=True),
    )
    row_count = tokens.shape[1]
    width = tokens.shape[2]
    head_count = width // 64
    per_group = min(4, head_count)
    group_count = head_count // per_group
    group_width = per_group * 64

    def to_groups(block):
        return jnp.transpose(block.reshape(block.shape[0], group_count, group_width), (1, 0, 2))

    def from_groups(block):
        return jnp.transpose(block, (1, 0, 2)).reshape(block.shape[1], width)

    residual_in = tokens[0].astype(jnp.float32)
    cosine_part, sine_part = rotary_tables(positions[:, 0, :])
    normed_in = norm_rows(
        residual_in, gathered[0].astype(jnp.float32), gathered[1].astype(jnp.float32)
    ).astype(jnp.bfloat16)
    projected = jnp.dot(normed_in, gathered[2], preferred_element_type=jnp.float32) + gathered[
        3
    ].astype(jnp.float32)
    queries = (
        rotate(projected[:, :width].reshape(row_count, head_count, 64), cosine_part, sine_part)
        .astype(jnp.bfloat16)
        .reshape(row_count, width)
    )
    keys = (
        rotate(
            projected[:, width : 2 * width].reshape(row_count, head_count, 64),
            cosine_part,
            sine_part,
        )
        .astype(jnp.bfloat16)
        .reshape(row_count, width)
    )
    values = projected[:, 2 * width :].astype(jnp.bfloat16)
    query_groups = to_groups(queries)
    key_all, value_all = (
        lax.all_gather(to_groups(keys), "seq", axis=1, tiled=True),
        lax.all_gather(to_groups(values), "seq", axis=1, tiled=True),
    )
    mixed, row_max, row_total = lax.map(attend, (query_groups, key_all, value_all))
    attended = from_groups(mixed).astype(jnp.bfloat16)
    residual_mid = residual_in + (
        jnp.dot(attended, gathered[4], preferred_element_type=jnp.float32)
        + gathered[5].astype(jnp.float32)
    )
    normed_mid = norm_rows(
        residual_mid, gathered[6].astype(jnp.float32), gathered[7].astype(jnp.float32)
    ).astype(jnp.bfloat16)
    upper = jnp.dot(normed_mid, gathered[8], preferred_element_type=jnp.float32) + gathered[
        9
    ].astype(jnp.float32)
    hidden = exact_gelu(upper).astype(jnp.bfloat16)
    result = residual_mid + (
        jnp.dot(hidden, gathered[10], preferred_element_type=jnp.float32)
        + gathered[11].astype(jnp.float32)
    )
    block_output = result.astype(jnp.bfloat16)[None]
    again = (
        lax.all_gather(shards[0], "fsdp", axis=0, tiled=True),
        lax.all_gather(shards[1], "fsdp", axis=0, tiled=True),
        lax.all_gather(shards[2], "fsdp", axis=0, tiled=True),
        lax.all_gather(shards[3], "fsdp", axis=0, tiled=True),
        lax.all_gather(shards[4], "fsdp", axis=0, tiled=True),
        lax.all_gather(shards[5], "fsdp", axis=0, tiled=True),
        lax.all_gather(shards[6], "fsdp", axis=0, tiled=True),
        lax.all_gather(shards[7], "fsdp", axis=0, tiled=True),
        lax.all_gather(shards[8], "fsdp", axis=0, tiled=True),
        lax.all_gather(shards[9], "fsdp", axis=0, tiled=True),
        lax.all_gather(shards[10], "fsdp", axis=0, tiled=True),
        lax.all_gather(shards[11], "fsdp", axis=0, tiled=True),
    )
    grad_low = cotangent[0]
    grad_out = grad_low.astype(jnp.float32)
    reduce_term = jnp.einsum("tf,td->fd", hidden, grad_low, preferred_element_type=jnp.float32)
    reduce_offset_term = jnp.sum(grad_out, axis=0)
    grad_hidden = jnp.einsum("td,fd->tf", grad_low, again[10], preferred_element_type=jnp.float32)
    gelu_pull = jax.vjp(exact_gelu, upper)[1]
    grad_upper = gelu_pull(grad_hidden)[0].astype(jnp.bfloat16)
    expand_term = jnp.einsum(
        "td,tf->df", normed_mid, grad_upper, preferred_element_type=jnp.float32
    )
    expand_offset_term = jnp.sum(grad_upper.astype(jnp.float32), axis=0)
    grad_mid_norm = jnp.einsum(
        "tf,df->td", grad_upper, again[8], preferred_element_type=jnp.float32
    )
    middle_pull = jax.vjp(
        norm_rows, residual_mid, again[6].astype(jnp.float32), again[7].astype(jnp.float32)
    )[1]
    grad_mid_in, middle_gain_term, middle_shift_term = middle_pull(grad_mid_norm)
    grad_resid = grad_out + grad_mid_in
    grad_branch = grad_resid.astype(jnp.bfloat16)
    output_term = jnp.einsum("td,te->de", attended, grad_branch, preferred_element_type=jnp.float32)
    output_offset_term = jnp.sum(grad_branch.astype(jnp.float32), axis=0)
    grad_attended = jnp.einsum(
        "te,de->td", grad_branch, again[4], preferred_element_type=jnp.float32
    ).astype(jnp.bfloat16)
    query_grad, key_grad, value_grad = lax.map(
        attend_back,
        (query_groups, key_all, value_all, to_groups(grad_attended), row_max, row_total),
    )
    key_share, value_share = (
        lax.psum_scatter(
            key_grad.astype(jnp.bfloat16), "seq", scatter_dimension=1, tiled=True
        ).astype(jnp.float32),
        lax.psum_scatter(
            value_grad.astype(jnp.bfloat16), "seq", scatter_dimension=1, tiled=True
        ).astype(jnp.float32),
    )
    grad_query = rotate(
        from_groups(query_grad).reshape(row_count, head_count, 64), cosine_part, -sine_part
    ).reshape(row_count, width)
    grad_key = rotate(
        from_groups(key_share).reshape(row_count, head_count, 64), cosine_part, -sine_part
    ).reshape(row_count, width)
    grad_value = from_groups(value_share)
    grad_projected = jnp.concatenate([grad_query, grad_key, grad_value], axis=1).astype(
        jnp.bfloat16
    )
    joint_term = jnp.einsum(
        "td,te->de", normed_in, grad_projected, preferred_element_type=jnp.float32
    )
    joint_offset_term = jnp.sum(grad_projected.astype(jnp.float32), axis=0)
    grad_in_norm = jnp.einsum(
        "te,de->td", grad_projected, again[2], preferred_element_type=jnp.float32
    )
    input_pull = jax.vjp(
        norm_rows, residual_in, again[0].astype(jnp.float32), again[1].astype(jnp.float32)
    )[1]
    grad_first_in, input_gain_term, input_shift_term = input_pull(grad_in_norm)
    input_gradient = (grad_resid + grad_first_in)[None]
    terms = (
        input_gain_term,
        input_shift_term,
        joint_term,
        joint_offset_term,
        output_term,
        output_offset_term,
        middle_gain_term,
        middle_shift_term,
        expand_term,
        expand_offset_term,
        reduce_term,
        reduce_offset_term,
    )
    owned = (
        lax.psum_scatter(
            terms[0].astype(jnp.bfloat16), "fsdp", scatter_dimension=0, tiled=True
        ).astype(jnp.float32),
        lax.psum_scatter(
            terms[1].astype(jnp.bfloat16), "fsdp", scatter_dimension=0, tiled=True
        ).astype(jnp.float32),
        lax.psum_scatter(
            terms[2].astype(jnp.bfloat16), "fsdp", scatter_dimension=0, tiled=True
        ).astype(jnp.float32),
        lax.psum_scatter(
            terms[3].astype(jnp.bfloat16), "fsdp", scatter_dimension=0, tiled=True
        ).astype(jnp.float32),
        lax.psum_scatter(
            terms[4].astype(jnp.bfloat16), "fsdp", scatter_dimension=0, tiled=True
        ).astype(jnp.float32),
        lax.psum_scatter(
            terms[5].astype(jnp.bfloat16), "fsdp", scatter_dimension=0, tiled=True
        ).astype(jnp.float32),
        lax.psum_scatter(
            terms[6].astype(jnp.bfloat16), "fsdp", scatter_dimension=0, tiled=True
        ).astype(jnp.float32),
        lax.psum_scatter(
            terms[7].astype(jnp.bfloat16), "fsdp", scatter_dimension=0, tiled=True
        ).astype(jnp.float32),
        lax.psum_scatter(
            terms[8].astype(jnp.bfloat16), "fsdp", scatter_dimension=0, tiled=True
        ).astype(jnp.float32),
        lax.psum_scatter(
            terms[9].astype(jnp.bfloat16), "fsdp", scatter_dimension=0, tiled=True
        ).astype(jnp.float32),
        lax.psum_scatter(
            terms[10].astype(jnp.bfloat16), "fsdp", scatter_dimension=0, tiled=True
        ).astype(jnp.float32),
        lax.psum_scatter(
            terms[11].astype(jnp.bfloat16), "fsdp", scatter_dimension=0, tiled=True
        ).astype(jnp.float32),
    )
    summed = (
        lax.psum(owned[0].astype(jnp.bfloat16), ("rep", "seq")).astype(jnp.float32),
        lax.psum(owned[1].astype(jnp.bfloat16), ("rep", "seq")).astype(jnp.float32),
        lax.psum(owned[2].astype(jnp.bfloat16), ("rep", "seq")).astype(jnp.float32),
        lax.psum(owned[3].astype(jnp.bfloat16), ("rep", "seq")).astype(jnp.float32),
        lax.psum(owned[4].astype(jnp.bfloat16), ("rep", "seq")).astype(jnp.float32),
        lax.psum(owned[5].astype(jnp.bfloat16), ("rep", "seq")).astype(jnp.float32),
        lax.psum(owned[6].astype(jnp.bfloat16), ("rep", "seq")).astype(jnp.float32),
        lax.psum(owned[7].astype(jnp.bfloat16), ("rep", "seq")).astype(jnp.float32),
        lax.psum(owned[8].astype(jnp.bfloat16), ("rep", "seq")).astype(jnp.float32),
        lax.psum(owned[9].astype(jnp.bfloat16), ("rep", "seq")).astype(jnp.float32),
        lax.psum(owned[10].astype(jnp.bfloat16), ("rep", "seq")).astype(jnp.float32),
        lax.psum(owned[11].astype(jnp.bfloat16), ("rep", "seq")).astype(jnp.float32),
    )
    return (
        block_output,
        input_gradient,
        summed[0],
        summed[1],
        summed[2],
        summed[3],
        summed[4],
        summed[5],
        summed[6],
        summed[7],
        summed[8],
        summed[9],
        summed[10],
        summed[11],
    )


def solution(mesh):
    return jax.shard_map(
        local,
        mesh=mesh,
        in_specs=(
            P(("rep", "fsdp"), "seq", None),
            P(None, ("rep", "fsdp"), "seq"),
            P("fsdp"),
            P("fsdp"),
            P("fsdp", None),
            P("fsdp"),
            P("fsdp", None),
            P("fsdp"),
            P("fsdp"),
            P("fsdp"),
            P("fsdp", None),
            P("fsdp"),
            P("fsdp", None),
            P("fsdp"),
            P(("rep", "fsdp"), "seq", None),
        ),
        out_specs=(
            P(("rep", "fsdp"), "seq", None),
            P(("rep", "fsdp"), "seq", None),
            P("fsdp"),
            P("fsdp"),
            P("fsdp", None),
            P("fsdp"),
            P("fsdp", None),
            P("fsdp"),
            P("fsdp"),
            P("fsdp"),
            P("fsdp", None),
            P("fsdp"),
            P("fsdp", None),
            P("fsdp"),
        ),
        check_vma=False,
    )
```

profile of v0, /device:TPU:0, one launch (start us, length us, event | category | flops | bytes accessed | tf_op | source)
XLA Modules:
  0.0 1273.0 jit_solution(16139119386478265900)
XLA Ops:
  8.6 14.8 %all-gather.2 = bf16[4,1,768]{2,1,0:T(2,128)(2,1)S(1)} all-gather(bf16[1,1,768]{2,1,0:T(2,128)(2,1)S(1)} %reshape.244), channel_id=1, replica_groups=mesh['rep'=4,'fsdp'=4,'seq'=2] {'fsdp'}, dimensions={0}, use_global_device_ids=true | all-gather | bytes 7680 | tf_op jit(solution)/shard_map/all_gather | solution.py:134
  24.2 12.4 all-gather.1
  37.3 8.0 all-gather
  46.8 1.6 fusion.22
  49.0 78.8 %all-gather.14.cloned.1.call-done = bf16[1024,3072]{1,0:T(8,128)(2,1)} async-done(((bf16[256,3072]{1,0:T(8,128)(2,1)}), bf16[1024,3072]{1,0:T(8,128)(2,1)}) %all-gather.14.cloned.1.call-update) | async-done | bytes 6291472 | tf_op jit(solution)/shard_map/all_gather | solution.py:133
  127.8 6.1 convolution_add_fusion
  133.9 2.6 copy-done.9
  139.2 4.9 fusion.45
  144.0 2.0 copy.83
  146.1 2.9 copy.87
  149.9 2.7 copy.88
  155.9 1.5 copy.90
  159.4 8.0 all-gather.3
  167.4 11.9 all_gather.59
  179.4 8.3 all-gather.5
  187.7 9.1 all-gather.4
  198.8 5.9 all-gather.18.cloned.1.call-done
  204.7 31.5 %while.30 = (s32[]{:T(128)}, bf16[4,512,256]{1,2,0:T(8,128)(2,1)S(1)}, f32[4,4,512,1]{2,1,3,0:T(4,128)S(1)}, f32[4,4,512,1]{2,1,3,0:T(4,128)S(1)}, bf16[4,1024,2...) while((s32[]{:T(128)}, ...), condition=%wide.region_5.6_spmd.clone, body=%wide.region_2.5_spmd.sunk.clone | while | flops 555741184 | bytes 29958248 | solution.py:185
  208.4 1.8 fusion.111
  210.2 2.3 fusion.112
  216.3 1.8 fusion.111
  218.1 2.3 fusion.112
  224.1 1.8 fusion.111
  225.9 2.3 fusion.112
  231.9 1.8 fusion.111
  233.8 2.3 fusion.112
  236.2 15.6 %all-gather.20.cloned.1.call-done = bf16[1024,1024]{1,0:T(8,128)(2,1)} async-done(((bf16[256,1024]{1,0:T(8,128)(2,1)}), bf16[1024,1024]{1,0:T(8,128)(2,1)}) %all-gather.20.cloned.1.call-update) | async-done | bytes 2097168 | tf_op jit(solution)/shard_map/all_gather | solution.py:135
  251.8 3.3 fusion.46
  255.5 146.2 %all-gather.22.cloned.1.call-done = bf16[1024,4096]{1,0:T(8,128)(2,1)} async-done(((bf16[256,4096]{1,0:T(8,128)(2,1)}), bf16[1024,4096]{1,0:T(8,128)(2,1)}) %all-gather.22.cloned.1.call-update) | async-done | bytes 8388624 | tf_op jit(solution)/shard_map/all_gather | solution.py:139
  401.7 27.6 %multiply_convert_fusion.1 = (bf16[512,4096]{1,0:T(8,128)(2,1)}, f32[512,4096]{1,0:T(8,128)}, f32[512,4096]{1,0:T(8,128)}) fusion(f32[4096]{0:T(1024)S(1)} %convert_element_type.220, bf16[1024,4096]{1,0:T(8,128)(2,1)} %all-gather.22.cloned.1.call-done, f32[512,1024]{1,0:T(8,128)S(1)} %get-tuple-element.210, f32[1024]{0:T(1024)S(1)} %bitcast.295, ...), kind=kOutput, calls=%fused_computation.31 | convolution fusion | flops 4436000768 | bytes 31485952 | tf_op jit(solution)/shard_map/dot_general | solution.py:194
  429.3 121.7 %all-gather.24.cloned.1.call-done = bf16[4096,1024]{1,0:T(8,128)(2,1)} async-done(((bf16[1024,1024]{1,0:T(8,128)(2,1)}), bf16[4096,1024]{1,0:T(8,128)(2,1)}) %all-gather.24.cloned.1.call-update) | async-done | bytes 8388624 | tf_op jit(solution)/shard_map/all_gather | solution.py:141
  550.9 15.9 %fusion.47 = (bf16[4096]{0:T(1024)(128)(2,1)}, bf16[512,4096]{1,0:T(8,128)(2,1)}) fusion(f32[512,4096]{1,0:T(8,128)} %get-tuple-element.179, bf16[4096,1024]{1,0:T(8,128)(2,1)} %all-gather.24.cloned.1.call-done, bf16[1,512,1024]{2,1,0:T(8,128)(2,1)S(1)} %copy-done.7, f32[512,4096]{1,0:T(8,128)} %get-tuple-element.211, f32[4096]{0:T(1024)S(1)} %convert_element_type.220), kind=kOutput, calls=%fused_computation.125 | convolution fusion | flops 4328517632 | bytes 30433280 | tf_op jit(solution)/shard_map/td,fd->tf/dot_general | solution.py:221
  566.9 7.6 multiply_reduce_fusion.2
  578.5 2.3 convolution_convert_fusion.4
  580.8 1.5 copy.99
  582.3 47.7 %while.31 = (s32[]{:T(128)}, f32[4,512,256]{1,2,0:T(8,128)S(1)}, bf16[4,1024,256]{1,2,0:T(8,128)(2,1)}, bf16[4,1024,256]{1,2,0:T(8,128)(2,1)}, bf16[4,1024,256]{...) while((s32[]{:T(128)}, f32[4,512,256]{1,2,0:T(8,128)S(1)}, ...), condition=%wide.region_12.13_spmd.clone, body=%wide.region_10.12_spmd.sunk.clone | while | flops 1361704960 | bytes 73465992 | solution.py:242
  584.6 2.5 exponential_divide_fusion.3
  587.1 1.5 multiply_reduce_fusion.10
  596.5 2.5 exponential_divide_fusion.3
  608.5 2.5 exponential_divide_fusion.3
  620.4 2.5 exponential_divide_fusion.3
  622.8 1.5 multiply_reduce_fusion.10
  632.0 3.8 convolution_convert_fusion.3
  636.2 2.8 copy.92
  639.0 21.3 %reduce-scatter.7.cloned.1.call-done = bf16[4,512,256]{1,2,0:T(8,128)(2,1)} async-done(((bf16[4,1024,256]{1,2,0:T(8,128)(2,1)}), bf16[4,512,256]{1,2,0:T(8,128)(2,1)}) %reduce-scatter.7.cloned.1.call-update) | async-done | bytes 1048592 | tf_op jit(solution)/shard_map/reduce_scatter | solution.py:247
  661.2 1.8 copy.101
  665.8 28.7 %reduce-scatter.9.cloned.1.call-done = bf16[4,512,256]{1,2,0:T(8,128)(2,1)} async-done(((bf16[4,1024,256]{1,2,0:T(8,128)(2,1)}), bf16[4,512,256]{1,2,0:T(8,128)(2,1)}) %reduce-scatter.9.cloned.1.call-update) | async-done | bytes 1048592 | tf_op jit(solution)/shard_map/reduce_scatter | solution.py:250
  694.5 7.7 convolution_convert_fusion.2
  702.3 1.7 copy-done.5
  704.0 9.2 convolution_convert_fusion.1
  713.5 10.4 convolution_convert_fusion
  724.5 11.5 all-gather.6
  740.5 112.2 %reduce-scatter.11.cloned.1.call-done = bf16[256,3072]{1,0:T(8,128)(2,1)} async-done(((bf16[1024,3072]{1,0:T(8,128)(2,1)}), bf16[256,3072]{1,0:T(8,128)(2,1)}) %reduce-scatter.11.cloned.1.call-update) | async-done | bytes 1572880 | tf_op jit(solution)/shard_map/reduce_scatter | solution.py:297
  852.7 147.5 %reduce-scatter.15.cloned.1.call-done = bf16[256,4096]{1,0:T(8,128)(2,1)} async-done(((bf16[1024,4096]{1,0:T(8,128)(2,1)}), bf16[256,4096]{1,0:T(8,128)(2,1)}) %reduce-scatter.15.cloned.1.call-update) | async-done | bytes 2097168 | tf_op jit(solution)/shard_map/reduce_scatter | solution.py:315
  1000.1 147.5 %reduce-scatter.17.cloned.1.call-done = bf16[1024,1024]{1,0:T(8,128)(2,1)} async-done(((bf16[4096,1024]{1,0:T(8,128)(2,1)}), bf16[1024,1024]{1,0:T(8,128)(2,1)}) %reduce-scatter.17.cloned.1.call-update) | async-done | bytes 2097168 | tf_op jit(solution)/shard_map/reduce_scatter | solution.py:321
  1147.7 10.3 fusion.24
  1157.9 6.8 fusion.40
  1167.2 18.9 %all-reduce.10 = (bf16[1024]{0:T(1024)(128)(2,1)S(1)}, bf16[1024]{0:T(1024)(128)(2,1)S(1)}, bf16[3072]{0:T(1024)(128)(2,1)S(1)}, bf16[1024]{0:T(1024)(128)(2,1)S...) all-reduce(bf16[1024]{0:T(1024)(128)(2,1)S(1)} %get-tuple-element.1, ...), channel_id=4, replica_groups=mesh['rep'=4,'fsdp'=4,'seq'=2] {'fsdp'}, use_global_device_ids=true, to_apply=%region_18.19.clone | all-reduce | flops 13312 | bytes 53248
  1186.6 14.8 %all-reduce.8 = (bf16[256]{0:T(256)(128)(2,1)S(1)}, bf16[256]{0:T(256)(128)(2,1)S(1)}, bf16[768]{0:T(1024)(128)(2,1)S(1)}, bf16[256]{0:T(256)(128)(2,1)S(1)}, bf...) all-reduce(bf16[256]{0:T(256)(128)(2,1)S(1)} %dynamic-slice.1, ...), channel_id=1, replica_groups=mesh['rep'=4,'fsdp'=4,'seq'=2] {'rep','seq'}, use_global_device_ids=true, to_apply=%region_19.20 | all-reduce | flops 3328 | bytes 13312 | tf_op jit(solution)/shard_map/psum | solution.py:329
  1206.0 4.1 add_bitcast_fusion
  1210.2 46.2 %all-reduce.13.cloned.1.call-done = (bf16[256,3072]{1,0:T(8,128)(2,1)}, bf16[256,1024]{1,0:T(8,128)(2,1)}, bf16[256,4096]{1,0:T(8,128)(2,1)}, bf16[1024,1024]{1,0:T(8,128)(2,1)}) async-done(((bf16[256,3072]{1,0:T(8,128)(2,1)}, bf16[256,1024]{1,0:T(8,128)(2,1)}, bf16[256,4096]{1,0:T(8,128)(2,1)}, bf16[1024,1024]{1,0:T(8,128)(2,1)}), (bf16[256,3072]{1,0:T(8,128)(2,1)}, bf16[256,1024]{1,0:T(8,128)(2,1)}, ...) | async-done | bytes 6291472 | tf_op jit(solution)/shard_map/psum | solution.py:331
  1256.4 3.6 convert_element_type.235
  1261.1 2.5 convert_element_type.245
  1263.6 2.5 convert_element_type.248
  (292 shorter events, 87.1 us)
Async XLA Ops:
  7.2 120.6 %all-gather.14.cloned.1.call-start = ((), (), s32[]{:S(2)}) async-start(), calls=%async_computation.6 | async-start | bytes 7864320 | tf_op jit(solution)/shard_map/all_gather | solution.py:133
  7.9 190.9 %all-gather.16.cloned.1.call-start = ((), (), s32[]{:S(2)}) async-start(), calls=%async_computation.7 | async-start | bytes 3145728 | tf_op jit(solution)/shard_map/all_gather | solution.py:183
  36.6 91.2 %copy-start.46 = (f32[4,1,256]{2,1,0:T(1,128)}, f32[4,1,256]{2,1,0:T(1,128)S(1)}, u32[]{:S(2)}) copy-start(f32[4,1,256]{2,1,0:T(1,128)S(1)} %convert_element_type.251) | copy-start | bytes 12292
  45.3 82.5 %copy-start.27 = (f32[4,1,256]{2,1,0:T(1,128)}, f32[4,1,256]{2,1,0:T(1,128)S(1)}, u32[]{:S(2)}) copy-start(f32[4,1,256]{2,1,0:T(1,128)S(1)} %convert_element_type.250) | copy-start | bytes 12292
  46.7 81.0 %copy-start.29 = (f32[512]{0:T(512)}, f32[512]{0:T(512)S(1)}, u32[]{:S(2)}) copy-start(f32[512]{0:T(512)S(1)} %broadcast_multiply_fusion.1) | copy-start | bytes 6148
  49.0 78.8 %copy-start.35 = (f32[512]{0:T(512)}, f32[512]{0:T(512)S(1)}, u32[]{:S(2)}) copy-start(f32[512]{0:T(512)S(1)} %fusion.32) | copy-start | bytes 6148
  133.9 2.6 copy-start.9
  138.0 66.7 %all-gather.18.cloned.1.call-start = ((), (), s32[]{:S(2)}) async-start(), calls=%async_computation.8 | async-start | bytes 3145728 | tf_op jit(solution)/shard_map/all_gather | solution.py:182
  139.2 14.6 %copy-start.23 = (f32[512,3,10]{0,2,1:T(8,128)}, f32[512,3,10]{0,2,1:T(8,128)S(1)}, u32[]{:S(2)}) copy-start(f32[512,3,10]{0,2,1:T(8,128)S(1)} %get-tuple-element.208) | copy-start | bytes 184324
  155.9 3.5 copy-start.54
  155.9 11.5 copy-start.50
  155.9 23.5 %copy-start.55 = (bf16[256]{0:T(256)(128)(2,1)S(1)}, bf16[256]{0:T(256)(128)(2,1)}, u32[]{:S(2)}) copy-start(bf16[256]{0:T(256)(128)(2,1)} %param.28) | copy-start | bytes 1540
  155.9 31.8 %copy-start.56 = (bf16[256]{0:T(256)(128)(2,1)S(1)}, bf16[256]{0:T(256)(128)(2,1)}, u32[]{:S(2)}) copy-start(bf16[256]{0:T(256)(128)(2,1)} %param.27) | copy-start | bytes 1540
  157.5 94.3 %all-gather.20.cloned.1.call-start = ((), (), s32[]{:S(2)}) async-start(), calls=%async_computation.9 | async-start | bytes 2621440 | tf_op jit(solution)/shard_map/all_gather | solution.py:135
  158.1 243.6 %all-gather.22.cloned.1.call-start = ((), (), s32[]{:S(2)}) async-start(), calls=%async_computation.10 | async-start | bytes 10485760 | tf_op jit(solution)/shard_map/all_gather | solution.py:139
  158.7 392.3 %all-gather.24.cloned.1.call-start = ((), (), s32[]{:S(2)}) async-start(), calls=%async_computation.11 | async-start | bytes 10485760 | tf_op jit(solution)/shard_map/all_gather | solution.py:141
  159.3 501.0 %reduce-scatter.7.cloned.1.call-start = ((), (), s32[]{:S(2)}) async-start(), calls=%async_computation.12 | async-start | bytes 3145728 | tf_op jit(solution)/shard_map/reduce_scatter | solution.py:247
  187.7 214.0 %copy-start.48 = (f32[4,1,256]{2,1,0:T(1,128)}, f32[4,1,256]{2,1,0:T(1,128)S(1)}, u32[]{:S(2)}) copy-start(f32[4,1,256]{2,1,0:T(1,128)S(1)} %convert_element_type.255) | copy-start | bytes 12292
  196.8 377.6 %copy-start.39 = (f32[4,1,256]{2,1,0:T(1,128)}, f32[4,1,256]{2,1,0:T(1,128)S(1)}, u32[]{:S(2)}) copy-start(f32[4,1,256]{2,1,0:T(1,128)S(1)} %convert_element_type.254) | copy-start | bytes 12292
  204.7 47.1 %copy-start = (bf16[1,512,1024]{2,1,0:T(8,128)(2,1)S(1)}, bf16[1,512,1024]{2,1,0:T(8,128)(2,1)}, u32[]{:S(2)}) copy-start(bf16[1,512,1024]{2,1,0:T(8,128)(2,1)} %param.19) | copy-start | bytes 3145732
  236.2 15.6 %copy-start.6 = (bf16[4,512,256]{1,2,0:T(8,128)(2,1)}, bf16[4,512,256]{1,2,0:T(8,128)(2,1)S(1)}, u32[]{:S(2)}) copy-start(bf16[4,512,256]{1,2,0:T(8,128)(2,1)S(1)} %get-tuple-element.471) | copy-start | bytes 3145732
  236.2 15.6 %copy-start.14 = (bf16[4,512,256]{1,2,0:T(8,128)(2,1)}, bf16[4,512,256]{1,2,0:T(8,128)(2,1)S(1)}, u32[]{:S(2)}) copy-start(bf16[4,512,256]{1,2,0:T(8,128)(2,1)S(1)} %get-tuple-element.107) | copy-start | bytes 3145732
  255.1 319.3 %copy-start.4 = (f32[512,1024]{1,0:T(8,128)}, f32[512,1024]{1,0:T(8,128)S(1)}, u32[]{:S(2)}) copy-start(f32[512,1024]{1,0:T(8,128)S(1)} %get-tuple-element.210) | copy-start | bytes 6291460
  255.1 319.3 %copy-start.37 = (f32[512]{0:T(512)}, f32[512]{0:T(512)S(1)}, u32[]{:S(2)}) copy-start(f32[512]{0:T(512)S(1)} %broadcast_multiply_fusion) | copy-start | bytes 6148
  255.5 319.0 %copy-start.42 = (f32[512]{0:T(512)}, f32[512]{0:T(512)S(1)}, u32[]{:S(2)}) copy-start(f32[512]{0:T(512)S(1)} %fusion.33) | copy-start | bytes 6148
  401.7 149.3 %copy-start.7 = (bf16[1,512,1024]{2,1,0:T(8,128)(2,1)S(1)}, bf16[1,512,1024]{2,1,0:T(8,128)(2,1)}, u32[]{:S(2)}) copy-start(bf16[1,512,1024]{2,1,0:T(8,128)(2,1)} %param.33) | copy-start | bytes 3145732
  550.9 15.9 %copy-start.53 = (bf16[1024,4096]{1,0:T(8,128)(2,1)S(1)}, bf16[1024,4096]{1,0:T(8,128)(2,1)}, u32[]{:S(2)}) copy-start(bf16[1024,4096]{1,0:T(8,128)(2,1)} %all-gather.22.cloned.1.call-done) | copy-start | bytes 25165828
  574.5 4.0 copy-start.20
  575.2 2.3 copy-start.31
  578.5 3.8 copy-start.16
  630.0 6.1 copy-start.17
  630.0 2.0 copy-start.15
  630.1 64.4 %reduce-scatter.9.cloned.1.call-start = ((), (), s32[]{:S(2)}) async-start(), calls=%async_computation.13 | async-start | bytes 3145728 | tf_op jit(solution)/shard_map/reduce_scatter | solution.py:250
  630.8 109.7 %reduce-scatter.13.cloned.1.call-start = ((), (), s32[]{:S(2)}) async-start(), calls=%async_computation.15 | async-start | bytes 2621440 | tf_op jit(solution)/shard_map/reduce_scatter | solution.py:303
  635.9 216.8 %reduce-scatter.11.cloned.1.call-start = ((), (), s32[]{:S(2)}) async-start(), calls=%async_computation.14 | async-start | bytes 7864320 | tf_op jit(solution)/shard_map/reduce_scatter | solution.py:297
  636.2 27.1 %copy-start.24 = (f32[512,3,10]{0,2,1:T(8,128)S(1)}, f32[512,3,10]{0,2,1:T(8,128)}, u32[]{:S(2)}) copy-start(f32[512,3,10]{0,2,1:T(8,128)} %copy-done.23) | copy-start | bytes 184324
  636.2 27.1 %copy-start.26 = (f32[512,3,10]{0,2,1:T(8,128)S(1)}, f32[512,3,10]{0,2,1:T(8,128)}, u32[]{:S(2)}) copy-start(f32[512,3,10]{0,2,1:T(8,128)} %get-tuple-element.206) | copy-start | bytes 184324
  664.3 30.2 %copy-start.1 = (bf16[1,512,1024]{2,1,0:T(8,128)(2,1)S(1)}, bf16[1,512,1024]{2,1,0:T(8,128)(2,1)}, u32[]{:S(2)}) copy-start(bf16[1,512,1024]{2,1,0:T(8,128)(2,1)} %param.19) | copy-start | bytes 3145732
  664.3 30.1 %copy-start.28 = (f32[4,1,256]{2,1,0:T(1,128)S(1)}, f32[4,1,256]{2,1,0:T(1,128)}, u32[]{:S(2)}) copy-start(f32[4,1,256]{2,1,0:T(1,128)} %copy-done.27) | copy-start | bytes 12292
  664.3 30.1 %copy-start.30 = (f32[512]{0:T(512)S(1)}, f32[512]{0:T(512)}, u32[]{:S(2)}) copy-start(f32[512]{0:T(512)} %copy-done.29) | copy-start | bytes 6148
  664.3 30.1 %copy-start.36 = (f32[512]{0:T(512)S(1)}, f32[512]{0:T(512)}, u32[]{:S(2)}) copy-start(f32[512]{0:T(512)} %copy-done.35) | copy-start | bytes 6148
  664.4 30.1 %copy-start.47 = (f32[4,1,256]{2,1,0:T(1,128)S(1)}, f32[4,1,256]{2,1,0:T(1,128)}, u32[]{:S(2)}) copy-start(f32[4,1,256]{2,1,0:T(1,128)} %copy-done.46) | copy-start | bytes 12292
  665.0 29.5 %copy-start.10 = (bf16[512,16,64]{0,2,1:T(8,128)(2,1)}, bf16[512,16,64]{0,2,1:T(8,128)(2,1)S(1)}, u32[]{:S(2)}) copy-start(bf16[512,16,64]{0,2,1:T(8,128)(2,1)S(1)} %copy.97) | copy-start | bytes 3145732
  665.8 28.7 %copy-start.12 = (bf16[512,16,64]{0,2,1:T(8,128)(2,1)}, bf16[512,16,64]{0,2,1:T(8,128)(2,1)S(1)}, u32[]{:S(2)}) copy-start(bf16[512,16,64]{0,2,1:T(8,128)(2,1)S(1)} %copy.94) | copy-start | bytes 3145732
  702.2 1.8 copy-start.38
  702.2 1.8 copy-start.40
  702.2 1.8 copy-start.43
  702.3 297.9 %reduce-scatter.15.cloned.1.call-start = ((), (), s32[]{:S(2)}) async-start(), calls=%async_computation.16 | async-start | bytes 10485760 | tf_op jit(solution)/shard_map/reduce_scatter | solution.py:315
  713.2 434.4 %reduce-scatter.17.cloned.1.call-start = ((), (), s32[]{:S(2)}) async-start(), calls=%async_computation.17 | async-start | bytes 10485760 | tf_op jit(solution)/shard_map/reduce_scatter | solution.py:321
  723.9 13.6 %copy-start.58 = (u32[32]{0:T(128)S(1)}, u32[32]{0:T(128)}, u32[]{:S(2)}) copy-start(u32[32]{0:T(128)} %constant.140) | copy-start | bytes 388
  723.9 532.5 %all-reduce.13.cloned.1.call-start = ((), (), s32[]{:S(2)}) async-start(), calls=%async_computation.18 | async-start | bytes 12582912 | tf_op jit(solution)/shard_map/psum | solution.py:331
  1147.6 10.3 copy-start.11
  1147.7 10.3 copy-start.13
  1147.7 10.3 copy-start.22
  1157.9 6.9 copy-start.34
  1164.8 2.3 copy-start.41
  1164.8 2.3 copy-start.44
  1164.8 2.3 copy-start.51
  1164.8 2.3 copy-start.52
  1164.8 41.2 %copy-start.3 = (f32[512,1024]{1,0:T(8,128)S(1)}, f32[512,1024]{1,0:T(8,128)}, u32[]{:S(2)}) copy-start(f32[512,1024]{1,0:T(8,128)} %copy-done.2) | copy-start | bytes 6291460
  1164.8 41.2 %copy-start.32 = (f32[512]{0:T(512)S(1)}, f32[512]{0:T(512)}, u32[]{:S(2)}) copy-start(f32[512]{0:T(512)} %copy-done.31) | copy-start | bytes 6148
  1256.4 3.6 copy-start.25
  1256.4 4.7 copy-start.19
  1260.0 3.6 copy-start.18
  (8 other events, 10.0 us)
Sparse Core Ops, SparseCore 0:
  9.6 118.1 all-gather.13
  138.1 31.2 all-gather.15
  171.6 33.0 all-gather.17
  206.1 45.6 all-gather.19
  253.2 148.4 all-gather.21
  403.1 147.7 all-gather.23
  630.2 30.0 reduce-scatter.6
  662.5 31.8 reduce-scatter.8
  696.8 43.6 reduce-scatter.12
  742.6 109.9 reduce-scatter.10
  855.0 145.0 reduce-scatter.14
  1002.3 145.2 reduce-scatter.16
  1151.2 105.1 all-reduce.12
where the time goes:
time: 1280 us; the launch traced here: 1270 us
  waiting for transfers between devices  875 us (68%)
  matrix products  154 us (12%)
  blocking collectives  118 us (9%)
  local copies, waits for them, and re-layouts  64 us (5%)
  other arithmetic  43.8 us (3%)
  between operations  17.1 us (1%)
    reduce_scatter x1, waiting for transfers between devices, local(): lax.psum_scatter(terms[8].astype(jnp.bfloat16), 'fsdp', scatter_dimension...  147 us
    reduce_scatter x1, waiting for transfers between devices, local(): lax.psum_scatter(terms[10].astype(jnp.bfloat16), 'fsdp', scatter_dimensio...  147 us
    all_gather x1, waiting for transfers between devices, local(): lax.all_gather(shards[8], 'fsdp', axis=0, tiled=True)  146 us
    all_gather x1, waiting for transfers between devices, local(): lax.all_gather(shards[10], 'fsdp', axis=0, tiled=True)  122 us
    reduce_scatter x1, waiting for transfers between devices, local(): lax.psum_scatter(terms[2].astype(jnp.bfloat16), 'fsdp', scatter_dimension...  112 us
    all_gather x1, waiting for transfers between devices, local(): lax.all_gather(shards[2], 'fsdp', axis=0, tiled=True)  78.8 us
    psum x1, waiting for transfers between devices, local(): lax.psum(owned[2].astype(jnp.bfloat16), ('rep', 'seq')).astype(jnp.float32)  46.2 us
    reduce_scatter x1, waiting for transfers between devices, local(): lax.psum_scatter(value_grad.astype(jnp.bfloat16), 'seq', scatter_dimensio...  28.7 us
  transfers between devices with their start and end apart: 13, of which 12 were waited for; matrix products, arithmetic and copies ran while one was open for 12% of the time, Pallas kernels for 0%

commit v1 on v0

--- a/solution.py
+++ b/solution.py
@@ -2,6 +2,7 @@
 import jax.numpy as jnp
 from jax import lax
 from jax.sharding import PartitionSpec as P
+from jax.lax import axis_index, axis_size, ppermute
 
 epsilon = 1e-06
 
@@ -113,6 +114,34 @@
     reduce_bias,
     cotangent,
 ):
+
+    def plane_manage(body):
+        odd = axis_size("fsdp")
+        right_arr, next_value, state_next = (odd, axis_index("fsdp"), body.shape[0])
+        in_order = [k * right_arr if hop_no == 0 else k for hop_no, k in enumerate(body.shape)]
+        spare = lax.dynamic_update_slice_in_dim(
+            jnp.zeros(in_order, body.dtype), body, next_value * state_next, axis=0
+        )
+        heard = x_new = body
+        for rr in range(1, right_arr // 2 + 1):
+            w1 = list(map(lambda hop_no: (hop_no, (hop_no + 1) % right_arr), range(right_arr)))
+            heard = ppermute(heard, axis_name="fsdp", perm=w1)
+            spare = lax.dynamic_update_slice_in_dim(
+                spare, heard, (next_value - rr) % right_arr * state_next, axis=0
+            )
+            if 2 * rr < right_arr:
+                x_new = ppermute(
+                    x_new,
+                    axis_name="fsdp",
+                    perm=list(
+                        map(lambda hop_no: (hop_no, (hop_no - 1) % right_arr), range(right_arr))
+                    ),
+                )
+                spare = lax.dynamic_update_slice_in_dim(
+                    spare, x_new, (next_value + rr) % right_arr * state_next, axis=0
+                )
+        return spare
+
     shards = (
         input_gain,
         input_shift,
@@ -136,7 +165,7 @@
         lax.all_gather(shards[5], "fsdp", axis=0, tiled=True),
         lax.all_gather(shards[6], "fsdp", axis=0, tiled=True),
         lax.all_gather(shards[7], "fsdp", axis=0, tiled=True),
-        lax.all_gather(shards[8], "fsdp", axis=0, tiled=True),
+        plane_manage(shards[8]),
         lax.all_gather(shards[9], "fsdp", axis=0, tiled=True),
         lax.all_gather(shards[10], "fsdp", axis=0, tiled=True),
         lax.all_gather(shards[11], "fsdp", axis=0, tiled=True),

time: 1280 us -> 1340 us (1.047)
  blocking collectives: 118 us -> 273 us
  waiting for transfers between devices: 875 us -> 758 us
  local copies, waits for them, and re-layouts: 64 us -> 78.4 us
    all_gather x1, blocking collectives: 7.97 us -> 151 us  [local(): lax.all_gather(shards[5], 'fsdp', axis=0, tiled=True)]
    all_gather x1, waiting for transfers between devices: 122 us -> 0.01 us  [local(): lax.all_gather(shards[10], 'fsdp', axis=0, tiled=True)]
    ppermute x0 -> x3, waiting for transfers between devices: none -> 46.8 us  [the longest x2 46.8 us: plane_manage(): heard = ppermute(heard, axis_name='fsdp', perm=w1)]
    all_gather x1, waiting for transfers between devices: 146 us -> 123 us  [local(): lax.all_gather(shards[8], 'fsdp', axis=0, tiled=True)]
    all_gather x1, waiting for transfers between devices: 15.6 us -> 0.02 us  [local(): lax.all_gather(shards[4], 'fsdp', axis=0, tiled=True)]
  transfers between devices with their start and end apart: 13 -> 16, of which waited for: 12 -> 10; matrix products, arithmetic and copies ran while one was open for 12% -> 13% of each run, Pallas kernels for 0% -> 0%
where the time goes in v1:
time: 1340 us; the launch traced here: 1330 us
  waiting for transfers between devices  758 us (57%)
  blocking collectives  273 us (20%)
  matrix products  153 us (11%)
  local copies, waits for them, and re-layouts  78.4 us (6%)
  other arithmetic  42.6 us (3%)
  between operations  17.3 us (1%)
    all_gather x1, blocking collectives, local(): lax.all_gather(shards[5], 'fsdp', axis=0, tiled=True)  151 us
    reduce_scatter x1, waiting for transfers between devices, local(): lax.psum_scatter(terms[8].astype(jnp.bfloat16), 'fsdp', scatter_dimension...  147 us
    reduce_scatter x1, waiting for transfers between devices, local(): lax.psum_scatter(terms[10].astype(jnp.bfloat16), 'fsdp', scatter_dimensio...  146 us
    all_gather x1, waiting for transfers between devices, local(): lax.all_gather(shards[8], 'fsdp', axis=0, tiled=True)  123 us
    reduce_scatter x1, waiting for transfers between devices, local(): lax.psum_scatter(terms[2].astype(jnp.bfloat16), 'fsdp', scatter_dimension...  114 us
    all_gather x1, waiting for transfers between devices, local(): lax.all_gather(shards[2], 'fsdp', axis=0, tiled=True)  78.8 us
    ppermute x2, waiting for transfers between devices, plane_manage(): heard = ppermute(heard, axis_name='fsdp', perm=w1)  46.8 us
    psum x1, waiting for transfers between devices, local(): lax.psum(owned[2].astype(jnp.bfloat16), ('rep', 'seq')).astype(jnp.float32)  46.2 us
  transfers between devices with their start and end apart: 16, of which 10 were waited for; matrix products, arithmetic and copies ran while one was open for 13% of the time, Pallas kernels for 0%

profile of v1, /device:TPU:0, one launch (start us, length us, event | category | flops | bytes accessed | tf_op | source)
XLA Modules:
  0.0 1327.5 jit_solution(15498730047374321025)
XLA Ops:
  8.6 14.8 %all-gather.2 = bf16[4,1,768]{2,1,0:T(2,128)(2,1)S(1)} all-gather(bf16[1,1,768]{2,1,0:T(2,128)(2,1)S(1)} %reshape.244), channel_id=1, replica_groups=mesh['rep'=4,'fsdp'=4,'seq'=2] {'fsdp'}, dimensions={0}, use_global_device_ids=true | all-gather | bytes 7680 | tf_op jit(solution)/shard_map/all_gather | solution.py:163
  24.2 12.4 all-gather.1
  37.3 8.0 all-gather
  46.8 1.6 fusion.22
  49.0 78.8 %all-gather.14.cloned.1.call-done = bf16[1024,3072]{1,0:T(8,128)(2,1)} async-done(((bf16[256,3072]{1,0:T(8,128)(2,1)}), bf16[1024,3072]{1,0:T(8,128)(2,1)}) %all-gather.14.cloned.1.call-update) | async-done | bytes 6291472 | tf_op jit(solution)/shard_map/all_gather | solution.py:162
  127.8 6.1 convolution_add_fusion
  133.9 2.6 copy-done.12
  139.2 4.9 fusion.45
  144.1 2.0 copy.83
  146.1 2.9 copy.87
  149.9 2.7 copy.88
  158.8 3.8 collective-permute-start.1
  162.6 46.8 %collective-permute-done = bf16[256,4096]{1,0:T(8,128)(2,1)} collective-permute-done((bf16[256,4096]{1,0:T(8,128)(2,1)}, bf16[256,4096]{1,0:T(8,128)(2,1)}, u32[]{:S(2)}, u32[]{:S(2)}) %collective-permute-start) | collective-permute-done | bytes 2097184 | tf_op jit(solution)/shard_map/ppermute | solution.py:128
  209.7 151.1 %all-gather.3 = bf16[4,1,256]{2,1,0:T(2,128)(2,1)S(1)} all-gather(bf16[1,1,256]{2,1,0:T(2,128)(2,1)S(1)} %reshape.246), channel_id=1, replica_groups=mesh['rep'=4,'fsdp'=4,'seq'=2] {'fsdp'}, dimensions={0}, use_global_device_ids=true | all-gather | bytes 2560 | tf_op jit(solution)/shard_map/all_gather | solution.py:165
  360.8 18.8 %all_gather.57 = bf16[4096]{0:T(1024)(128)(2,1)S(1)} all-gather(bf16[1024]{0:T(1024)(128)(2,1)S(1)} %copy-done.51), channel_id=1, replica_groups=mesh['rep'=4,'fsdp'=4,'seq'=2] {'fsdp'}, dimensions={0}, use_global_device_ids=true | all-gather | bytes 10240 | tf_op jit(solution)/shard_map/all_gather | solution.py:169
  379.6 11.3 all-gather.5
  390.9 11.3 all-gather.4
  404.2 1.9 constant_dynamic-update-slice_fusion.6
  406.1 2.0 constant_dynamic-update-slice_fusion.5
  408.1 1.9 constant_dynamic-update-slice_fusion.4
  410.0 3.2 copy-done.9
  414.0 31.6 %while.30 = (s32[]{:T(128)}, bf16[4,512,256]{1,2,0:T(8,128)(2,1)S(1)}, f32[4,4,512,1]{2,1,3,0:T(4,128)S(1)}, f32[4,4,512,1]{2,1,3,0:T(4,128)S(1)}, bf16[4,1024,2...) while((s32[]{:T(128)}, ...), condition=%wide.region_5.6_spmd.clone, body=%wide.region_2.5_spmd.sunk.clone | while | flops 555741184 | bytes 29958248 | solution.py:214
  417.9 1.8 fusion.111
  419.7 2.3 fusion.112
  425.7 1.8 fusion.111
  427.6 2.3 fusion.112
  433.6 1.8 fusion.111
  435.4 2.3 fusion.112
  441.4 1.8 fusion.111
  443.2 2.3 fusion.112
  447.0 3.4 fusion.46
  451.3 26.3 %multiply_convert_fusion.1 = (bf16[512,4096]{1,0:T(8,128)(2,1)}, f32[512,4096]{1,0:T(8,128)}, f32[512,4096]{1,0:T(8,128)}) fusion(f32[4096]{0:T(1024)S(1)} %convert_element_type.220, bf16[1024,4096]{1,0:T(8,128)(2,1)S(1)} %copy-done.10, f32[512,1024]{1,0:T(8,128)S(1)} %get-tuple-element.210, f32[1024]{0:T(1024)S(1)} %bitcast.295, f32[1024]{0:T(1024)S(1)} %bitcast.288, ...), kind=kOutput, calls=%fused_computation.31 | convolution fusion | flops 4436000768 | bytes 31485952 | tf_op jit(solution)/shard_map/dot_general | solution.py:223
  477.6 16.3 %fusion.47 = (bf16[4096]{0:T(1024)(128)(2,1)}, bf16[512,4096]{1,0:T(8,128)(2,1)}) fusion(f32[512,4096]{1,0:T(8,128)} %get-tuple-element.179, bf16[4096,1024]{1,0:T(8,128)(2,1)} %all-gather.22.cloned.1.call-done, bf16[1,512,1024]{2,1,0:T(8,128)(2,1)S(1)} %copy-done.7, f32[512,4096]{1,0:T(8,128)} %get-tuple-element.211, f32[4096]{0:T(1024)S(1)} %convert_element_type.220), kind=kOutput, calls=%fused_computation.129 | convolution fusion | flops 4328517632 | bytes 30433280 | tf_op jit(solution)/shard_map/td,fd->tf/dot_general | solution.py:250
  493.9 123.4 %all-gather.24.cloned.1.call-done = bf16[1024,4096]{1,0:T(8,128)(2,1)} async-done(((bf16[256,4096]{1,0:T(8,128)(2,1)}), bf16[1024,4096]{1,0:T(8,128)(2,1)}) %all-gather.24.cloned.1.call-update) | async-done | bytes 8388624 | tf_op jit(solution)/shard_map/all_gather | solution.py:241
  617.3 9.3 multiply_reduce_fusion.2
  629.7 2.3 convolution_convert_fusion.4
  633.4 51.1 %while.31 = (s32[]{:T(128)}, f32[4,512,256]{1,2,0:T(8,128)}, bf16[4,1024,256]{1,2,0:T(8,128)(2,1)}, bf16[4,1024,256]{1,2,0:T(8,128)(2,1)}, bf16[4,1024,256]{1,2,...) while((s32[]{:T(128)}, f32[4,512,256]{1,2,0:T(8,128)}, ...), condition=%wide.region_12.13_spmd.clone, body=%wide.region_10.12_spmd.sunk.clone | while | flops 1361704960 | bytes 73465992 | solution.py:271
  635.9 2.5 exponential_divide_fusion.3
  648.6 2.4 exponential_divide_fusion.3
  661.3 2.4 exponential_divide_fusion.3
  674.0 2.4 exponential_divide_fusion.3
  685.7 2.6 convolution_convert_fusion.3
  688.4 9.6 convolution_convert_fusion
  699.3 2.8 copy.92
  702.1 12.7 reduce-scatter.7.cloned.1.call-done
  715.7 1.8 copy.101
  720.2 28.7 %reduce-scatter.9.cloned.1.call-done = bf16[4,512,256]{1,2,0:T(8,128)(2,1)} async-done(((bf16[4,1024,256]{1,2,0:T(8,128)(2,1)}), bf16[4,512,256]{1,2,0:T(8,128)(2,1)}) %reduce-scatter.9.cloned.1.call-update) | async-done | bytes 1048592 | tf_op jit(solution)/shard_map/reduce_scatter | solution.py:279
  749.0 7.7 convolution_convert_fusion.2
  756.7 1.7 copy-done.5
  758.5 9.2 convolution_convert_fusion.1
  769.2 11.7 all-gather.6
  783.4 11.5 reduce-scatter.13.cloned.1.call-done
  795.0 146.1 %reduce-scatter.17.cloned.1.call-done = bf16[1024,1024]{1,0:T(8,128)(2,1)} async-done(((bf16[4096,1024]{1,0:T(8,128)(2,1)}), bf16[1024,1024]{1,0:T(8,128)(2,1)}) %reduce-scatter.17.cloned.1.call-update) | async-done | bytes 2097168 | tf_op jit(solution)/shard_map/reduce_scatter | solution.py:350
  941.0 113.7 %reduce-scatter.11.cloned.1.call-done = bf16[256,3072]{1,0:T(8,128)(2,1)} async-done(((bf16[1024,3072]{1,0:T(8,128)(2,1)}), bf16[256,3072]{1,0:T(8,128)(2,1)}) %reduce-scatter.11.cloned.1.call-update) | async-done | bytes 1572880 | tf_op jit(solution)/shard_map/reduce_scatter | solution.py:326
  1054.8 147.4 %reduce-scatter.15.cloned.1.call-done = bf16[256,4096]{1,0:T(8,128)(2,1)} async-done(((bf16[1024,4096]{1,0:T(8,128)(2,1)}), bf16[256,4096]{1,0:T(8,128)(2,1)}) %reduce-scatter.15.cloned.1.call-update) | async-done | bytes 2097168 | tf_op jit(solution)/shard_map/reduce_scatter | solution.py:344
  1202.2 10.3 fusion.24
  1212.4 6.8 fusion.40
  1221.7 18.9 %all-reduce.10 = (bf16[1024]{0:T(1024)(128)(2,1)S(1)}, bf16[1024]{0:T(1024)(128)(2,1)S(1)}, bf16[3072]{0:T(1024)(128)(2,1)S(1)}, bf16[1024]{0:T(1024)(128)(2,1)S...) all-reduce(bf16[1024]{0:T(1024)(128)(2,1)S(1)} %get-tuple-element.1, ...), channel_id=4, replica_groups=mesh['rep'=4,'fsdp'=4,'seq'=2] {'fsdp'}, use_global_device_ids=true, to_apply=%region_18.19.clone | all-reduce | flops 13312 | bytes 53248
  1241.1 14.9 %all-reduce.8 = (bf16[256]{0:T(256)(128)(2,1)S(1)}, bf16[256]{0:T(256)(128)(2,1)S(1)}, bf16[768]{0:T(1024)(128)(2,1)S(1)}, bf16[256]{0:T(256)(128)(2,1)S(1)}, bf...) all-reduce(bf16[256]{0:T(256)(128)(2,1)S(1)} %dynamic-slice.1, ...), channel_id=1, replica_groups=mesh['rep'=4,'fsdp'=4,'seq'=2] {'rep','seq'}, use_global_device_ids=true, to_apply=%region_19.20 | all-reduce | flops 3328 | bytes 13312 | tf_op jit(solution)/shard_map/psum | solution.py:358
  1260.6 4.1 add_bitcast_fusion
  1264.7 46.2 %all-reduce.13.cloned.1.call-done = (bf16[256,3072]{1,0:T(8,128)(2,1)}, bf16[256,1024]{1,0:T(8,128)(2,1)}, bf16[256,4096]{1,0:T(8,128)(2,1)}, bf16[1024,1024]{1,0:T(8,128)(2,1)}) async-done(((bf16[256,3072]{1,0:T(8,128)(2,1)}, bf16[256,1024]{1,0:T(8,128)(2,1)}, bf16[256,4096]{1,0:T(8,128)(2,1)}, bf16[1024,1024]{1,0:T(8,128)(2,1)}), (bf16[256,3072]{1,0:T(8,128)(2,1)}, bf16[256,1024]{1,0:T(8,128)(2,1)}, ...) | async-done | bytes 6291472 | tf_op jit(solution)/shard_map/psum | solution.py:360
  1310.9 3.6 convert_element_type.235
  1315.6 2.5 convert_element_type.245
  1318.1 2.5 convert_element_type.248
  (303 shorter events, 96.2 us)
Async XLA Ops:
  7.2 120.6 %all-gather.14.cloned.1.call-start = ((), (), s32[]{:S(2)}) async-start(), calls=%async_computation.6 | async-start | bytes 7864320 | tf_op jit(solution)/shard_map/all_gather | solution.py:162
  7.9 406.0 %all-gather.16.cloned.1.call-start = ((), (), s32[]{:S(2)}) async-start(), calls=%async_computation.7 | async-start | bytes 3145728 | tf_op jit(solution)/shard_map/all_gather | solution.py:212
  36.6 91.2 %copy-start.47 = (f32[4,1,256]{2,1,0:T(1,128)}, f32[4,1,256]{2,1,0:T(1,128)S(1)}, u32[]{:S(2)}) copy-start(f32[4,1,256]{2,1,0:T(1,128)S(1)} %convert_element_type.251) | copy-start | bytes 12292
  45.3 82.5 %copy-start.28 = (f32[4,1,256]{2,1,0:T(1,128)}, f32[4,1,256]{2,1,0:T(1,128)S(1)}, u32[]{:S(2)}) copy-start(f32[4,1,256]{2,1,0:T(1,128)S(1)} %convert_element_type.250) | copy-start | bytes 12292
  46.7 81.0 %copy-start.30 = (f32[512]{0:T(512)}, f32[512]{0:T(512)S(1)}, u32[]{:S(2)}) copy-start(f32[512]{0:T(512)S(1)} %broadcast_multiply_fusion.1) | copy-start | bytes 6148
  49.0 78.8 %copy-start.36 = (f32[512]{0:T(512)}, f32[512]{0:T(512)S(1)}, u32[]{:S(2)}) copy-start(f32[512]{0:T(512)S(1)} %fusion.32) | copy-start | bytes 6148
  133.9 2.6 copy-start.12
  138.0 275.9 %all-gather.18.cloned.1.call-start = ((), (), s32[]{:S(2)}) async-start(), calls=%async_computation.8 | async-start | bytes 3145728 | tf_op jit(solution)/shard_map/all_gather | solution.py:211
  139.2 14.6 %copy-start.24 = (f32[512,3,10]{0,2,1:T(8,128)}, f32[512,3,10]{0,2,1:T(8,128)S(1)}, u32[]{:S(2)}) copy-start(f32[512,3,10]{0,2,1:T(8,128)S(1)} %get-tuple-element.208) | copy-start | bytes 184324
  155.9 53.7 %copy-start.54 = (bf16[256]{0:T(256)(128)(2,1)S(1)}, bf16[256]{0:T(256)(128)(2,1)}, u32[]{:S(2)}) copy-start(bf16[256]{0:T(256)(128)(2,1)} %param.26) | copy-start | bytes 1540
  155.9 204.8 %copy-start.51 = (bf16[1024]{0:T(1024)(128)(2,1)S(1)}, bf16[1024]{0:T(1024)(128)(2,1)}, u32[]{:S(2)}) copy-start(bf16[1024]{0:T(1024)(128)(2,1)} %param.30) | copy-start | bytes 6148
  155.9 223.6 %copy-start.55 = (bf16[256]{0:T(256)(128)(2,1)S(1)}, bf16[256]{0:T(256)(128)(2,1)}, u32[]{:S(2)}) copy-start(bf16[256]{0:T(256)(128)(2,1)} %param.28) | copy-start | bytes 1540
  155.9 235.0 %copy-start.56 = (bf16[256]{0:T(256)(128)(2,1)S(1)}, bf16[256]{0:T(256)(128)(2,1)}, u32[]{:S(2)}) copy-start(bf16[256]{0:T(256)(128)(2,1)} %param.27) | copy-start | bytes 1540
  157.5 288.2 %all-gather.20.cloned.1.call-start = ((), (), s32[]{:S(2)}) async-start(), calls=%async_computation.9 | async-start | bytes 2621440 | tf_op jit(solution)/shard_map/all_gather | solution.py:164
  158.1 319.5 %all-gather.22.cloned.1.call-start = ((), (), s32[]{:S(2)}) async-start(), calls=%async_computation.10 | async-start | bytes 10485760 | tf_op jit(solution)/shard_map/all_gather | solution.py:170
  158.7 458.6 %all-gather.24.cloned.1.call-start = ((), (), s32[]{:S(2)}) async-start(), calls=%async_computation.11 | async-start | bytes 10485760 | tf_op jit(solution)/shard_map/all_gather | solution.py:241
  158.7 50.7 %collective-permute-start = (bf16[256,4096]{1,0:T(8,128)(2,1)}, bf16[256,4096]{1,0:T(8,128)(2,1)}, u32[]{:S(2)}, u32[]{:S(2)}) collective-permute-start(bf16[256,4096]{1,0:T(8,128)(2,1)} %param.29), channel_id=1, source_target_pairs={{0,2},{2,4},{4,6},{6,0},{1,3},{3,5},{5,7},{7,1},{8,10},{10,12},{12... | collective-permute-start | bytes 6291464 | tf_op jit(solution)/shard_map/ppermute | solution.py:128
  158.8 247.3 %collective-permute-start.1 = (bf16[256,4096]{1,0:T(8,128)(2,1)}, bf16[256,4096]{1,0:T(8,128)(2,1)}, u32[]{:S(2)}, u32[]{:S(2)}) collective-permute-start(bf16[256,4096]{1,0:T(8,128)(2,1)} %param.29), channel_id=1, source_target_pairs={{0,6},{2,0},{4,2},{6,4},{1,7},{3,1},{5,3},{7,5},{8,14},{10,8},{12,... | collective-permute-start | bytes 6291464 | tf_op jit(solution)/shard_map/ppermute | solution.py:133
  209.4 198.6 %collective-permute-start.2 = (bf16[256,4096]{1,0:T(8,128)(2,1)}, bf16[256,4096]{1,0:T(8,128)(2,1)}, u32[]{:S(2)}, u32[]{:S(2)}) collective-permute-start(bf16[256,4096]{1,0:T(8,128)(2,1)} %collective-permute-done), channel_id=1, source_target_pairs={{0,2},{2,4},{4,6},{6,0},{1,3},{3,5},{5,7},{7,1},{8,10},{10,12},{12... | collective-permute-start | bytes 6291464 | tf_op jit(solution)/shard_map/ppermute | solution.py:128
  209.5 505.3 %reduce-scatter.7.cloned.1.call-start = ((), (), s32[]{:S(2)}) async-start(), calls=%async_computation.12 | async-start | bytes 3145728 | tf_op jit(solution)/shard_map/reduce_scatter | solution.py:276
  390.9 59.9 %copy-start.49 = (f32[4,1,256]{2,1,0:T(1,128)}, f32[4,1,256]{2,1,0:T(1,128)S(1)}, u32[]{:S(2)}) copy-start(f32[4,1,256]{2,1,0:T(1,128)S(1)} %convert_element_type.255) | copy-start | bytes 12292
  402.2 224.4 %copy-start.40 = (f32[4,1,256]{2,1,0:T(1,128)}, f32[4,1,256]{2,1,0:T(1,128)S(1)}, u32[]{:S(2)}) copy-start(f32[4,1,256]{2,1,0:T(1,128)S(1)} %convert_element_type.254) | copy-start | bytes 12292
  406.1 7.2 copy-start.19
  410.0 3.3 copy-start.9
  414.0 33.0 %copy-start = (bf16[1,512,1024]{2,1,0:T(8,128)(2,1)S(1)}, bf16[1,512,1024]{2,1,0:T(8,128)(2,1)}, u32[]{:S(2)}) copy-start(bf16[1,512,1024]{2,1,0:T(8,128)(2,1)} %param.19) | copy-start | bytes 3145732
  447.0 4.3 copy-start.10
  450.4 176.2 %copy-start.4 = (f32[512,1024]{1,0:T(8,128)}, f32[512,1024]{1,0:T(8,128)S(1)}, u32[]{:S(2)}) copy-start(f32[512,1024]{1,0:T(8,128)S(1)} %get-tuple-element.210) | copy-start | bytes 6291460
  450.4 176.2 %copy-start.38 = (f32[512]{0:T(512)}, f32[512]{0:T(512)S(1)}, u32[]{:S(2)}) copy-start(f32[512]{0:T(512)S(1)} %broadcast_multiply_fusion) | copy-start | bytes 6148
  450.8 175.8 %copy-start.43 = (f32[512]{0:T(512)}, f32[512]{0:T(512)S(1)}, u32[]{:S(2)}) copy-start(f32[512]{0:T(512)S(1)} %fusion.33) | copy-start | bytes 6148
  451.3 26.3 %copy-start.7 = (bf16[1,512,1024]{2,1,0:T(8,128)(2,1)S(1)}, bf16[1,512,1024]{2,1,0:T(8,128)(2,1)}, u32[]{:S(2)}) copy-start(bf16[1,512,1024]{2,1,0:T(8,128)(2,1)} %param.33) | copy-start | bytes 3145732
  626.6 3.0 copy-start.22
  627.4 4.5 copy-start.32
  684.5 64.4 %reduce-scatter.9.cloned.1.call-start = ((), (), s32[]{:S(2)}) async-start(), calls=%async_computation.13 | async-start | bytes 3145728 | tf_op jit(solution)/shard_map/reduce_scatter | solution.py:279
  685.3 109.7 %reduce-scatter.13.cloned.1.call-start = ((), (), s32[]{:S(2)}) async-start(), calls=%async_computation.15 | async-start | bytes 2621440 | tf_op jit(solution)/shard_map/reduce_scatter | solution.py:332
  688.3 252.7 %reduce-scatter.17.cloned.1.call-start = ((), (), s32[]{:S(2)}) async-start(), calls=%async_computation.17 | async-start | bytes 10485760 | tf_op jit(solution)/shard_map/reduce_scatter | solution.py:350
  698.0 356.7 %reduce-scatter.11.cloned.1.call-start = ((), (), s32[]{:S(2)}) async-start(), calls=%async_computation.14 | async-start | bytes 7864320 | tf_op jit(solution)/shard_map/reduce_scatter | solution.py:326
  699.3 18.5 %copy-start.25 = (f32[512,3,10]{0,2,1:T(8,128)S(1)}, f32[512,3,10]{0,2,1:T(8,128)}, u32[]{:S(2)}) copy-start(f32[512,3,10]{0,2,1:T(8,128)} %copy-done.24) | copy-start | bytes 184324
  699.3 18.5 %copy-start.27 = (f32[512,3,10]{0,2,1:T(8,128)S(1)}, f32[512,3,10]{0,2,1:T(8,128)}, u32[]{:S(2)}) copy-start(f32[512,3,10]{0,2,1:T(8,128)} %get-tuple-element.206) | copy-start | bytes 184324
  718.8 30.2 %copy-start.1 = (bf16[1,512,1024]{2,1,0:T(8,128)(2,1)S(1)}, bf16[1,512,1024]{2,1,0:T(8,128)(2,1)}, u32[]{:S(2)}) copy-start(bf16[1,512,1024]{2,1,0:T(8,128)(2,1)} %param.19) | copy-start | bytes 3145732
  718.8 30.1 %copy-start.29 = (f32[4,1,256]{2,1,0:T(1,128)S(1)}, f32[4,1,256]{2,1,0:T(1,128)}, u32[]{:S(2)}) copy-start(f32[4,1,256]{2,1,0:T(1,128)} %copy-done.28) | copy-start | bytes 12292
  718.8 30.1 %copy-start.31 = (f32[512]{0:T(512)S(1)}, f32[512]{0:T(512)}, u32[]{:S(2)}) copy-start(f32[512]{0:T(512)} %copy-done.30) | copy-start | bytes 6148
  718.8 30.1 %copy-start.37 = (f32[512]{0:T(512)S(1)}, f32[512]{0:T(512)}, u32[]{:S(2)}) copy-start(f32[512]{0:T(512)} %copy-done.36) | copy-start | bytes 6148
  718.8 30.1 %copy-start.48 = (f32[4,1,256]{2,1,0:T(1,128)S(1)}, f32[4,1,256]{2,1,0:T(1,128)}, u32[]{:S(2)}) copy-start(f32[4,1,256]{2,1,0:T(1,128)} %copy-done.47) | copy-start | bytes 12292
  719.4 29.5 %copy-start.13 = (bf16[512,16,64]{0,2,1:T(8,128)(2,1)}, bf16[512,16,64]{0,2,1:T(8,128)(2,1)S(1)}, u32[]{:S(2)}) copy-start(bf16[512,16,64]{0,2,1:T(8,128)(2,1)S(1)} %copy.97) | copy-start | bytes 3145732
  720.2 28.7 %copy-start.15 = (bf16[512,16,64]{0,2,1:T(8,128)(2,1)}, bf16[512,16,64]{0,2,1:T(8,128)(2,1)S(1)}, u32[]{:S(2)}) copy-start(bf16[512,16,64]{0,2,1:T(8,128)(2,1)S(1)} %copy.94) | copy-start | bytes 3145732
  756.6 1.8 copy-start.39
  756.6 1.8 copy-start.41
  756.6 1.8 copy-start.44
  756.7 445.4 %reduce-scatter.15.cloned.1.call-start = ((), (), s32[]{:S(2)}) async-start(), calls=%async_computation.16 | async-start | bytes 10485760 | tf_op jit(solution)/shard_map/reduce_scatter | solution.py:344
  767.7 13.2 copy-start.58
  767.7 543.2 %all-reduce.13.cloned.1.call-start = ((), (), s32[]{:S(2)}) async-start(), calls=%async_computation.18 | async-start | bytes 12582912 | tf_op jit(solution)/shard_map/psum | solution.py:360
  1202.1 10.3 copy-start.14
  1202.2 10.3 copy-start.16
  1202.2 10.3 copy-start.23
  1212.4 6.9 copy-start.35
  1219.3 2.3 copy-start.42
  1219.3 2.3 copy-start.45
  1219.3 2.3 copy-start.52
  1219.3 2.3 copy-start.53
  1219.3 41.2 %copy-start.3 = (f32[512,1024]{1,0:T(8,128)S(1)}, f32[512,1024]{1,0:T(8,128)}, u32[]{:S(2)}) copy-start(f32[512,1024]{1,0:T(8,128)} %copy-done.2) | copy-start | bytes 6291460
  1219.3 41.2 %copy-start.33 = (f32[512]{0:T(512)S(1)}, f32[512]{0:T(512)}, u32[]{:S(2)}) copy-start(f32[512]{0:T(512)} %copy-done.32) | copy-start | bytes 6148
  1310.9 3.6 copy-start.26
  1310.9 4.7 copy-start.21
  1314.5 3.6 copy-start.20
  (11 other events, 15.0 us)
Sparse Core Ops, SparseCore 0:
  9.6 118.1 all-gather.13
  138.2 31.2 all-gather.15
  171.6 33.0 all-gather.17
  206.1 75.7 all-gather.19
  283.4 184.4 all-gather.21
  469.3 147.9 all-gather.23
  684.6 30.0 reduce-scatter.6
  717.0 31.8 reduce-scatter.8
  751.2 43.6 reduce-scatter.12
  797.2 143.8 reduce-scatter.16
  943.3 111.3 reduce-scatter.10
  1057.0 145.1 reduce-scatter.14
  1205.7 105.1 all-reduce.12
